TPU v7x, 512 devices: a whole 4x4x16 slice. The times are simulated.
512 devices in a mesh: cfg: 2 (over core), grp: 4 (over y), seq: 64 (over x, z).
Axes of the slice: x: 4, y: 4, z: 16, core: 2. Of those that a mesh axis runs over, the one named last changes fastest.
Arguments:
- query: bfloat16 [2, 4, 2, 128, 2432], P('cfg', 'grp', None, 'seq'), may hold values from -150 to 150
- keys: bfloat16 [2, 4, 2, 128, 2432], P('cfg', 'grp', None, 'seq'), may hold values from -5.5 to 5.5
- values: bfloat16 [2, 4, 2, 128, 2432], P('cfg', 'grp', None, 'seq'), may hold values from -5 to 5
- hidden: bfloat16 [2, 4, 2, 128, 2432], P('cfg', 'grp', None, 'seq'), may hold values from -23 to 23
- latent: float32 [4, 2, 128, 64], P('grp', None, 'seq', 'cfg'), may hold values from -6 to 6
- deal: int32 [4, 2], replicated, may hold values from 0 to 5, as said below
- lengths: int32 [4, 2], replicated, may hold values from 64 to 128, as said below
- w_out: bfloat16 [2432, 2432], P(('cfg', 'seq')), may hold values from -0.125 to 0.125
- attn_gate: float32 [2, 6, 2432], P('cfg'), may hold values from 0.25 to 1.75
- modulation: float32 [2, 6, 2, 2432], P('cfg'), may hold values from -3 to 3
- w_final: bfloat16 [2432, 64], replicated, may hold values from -0.125 to 0.125
- guide: float32 [6], replicated, may hold values from 2 to 7
- step_size: float32 [6], replicated, may hold values from 0.15 to 0.5
Outputs:
- latent_next: float32 [4, 2, 128, 64], P('grp', None, 'seq', 'cfg')
Inputs may be any that keep to these rules, and one draw needn't show every extreme that they name: `deal`: column 0 of row g names the whole item of group g, column 1 the item split between groups g and g xor 1 (equal in both rows); every one of the 6 items is named by exactly one column-0 entry or one pair of column-1 entries. `lengths`: in each column some group has all 128 slots live.
All inputs are finite; a program needn't handle non-finite values.
Results may differ from a plain program's by a relative error of at most 0.0049.
Values may be sent and summed in bfloat16 or wider, within the bound.
No kernel may reach another device: no remote copies, remote signals or barrier semaphores. Data moves between devices by JAX's collectives and lax.ppermute only.
A program may use at most 128 MiB of HBM per device.

v0:
```python
import jax
import jax.numpy as jnp
from jax import lax
from jax.sharding import PartitionSpec as P

D = 2432
HEADS = 38
HD = 64
NORM_EPS = 1e-06


def from_partner(x, axis, apart):
    return lax.ppermute(x, axis, [(i, i ^ 1 << apart) for i in range(lax.axis_size(axis))])


def attend(queries, keys_all, values_all, live_keys):
    row_count = queries.shape[0]
    query_heads = queries.reshape(row_count, HEADS, HD)
    key_heads = keys_all.reshape(-1, HEADS, HD)
    value_heads = values_all.reshape(-1, HEADS, HD)
    scores = jnp.einsum(
        "shd,khd->hsk", query_heads, key_heads, preferred_element_type=jnp.float32
    ) * HD ** (-0.5)
    scores = jnp.where(live_keys[None, None, :], scores, -jnp.inf)
    peak_score = jnp.max(scores, axis=2, keepdims=True)
    raw_weights = jnp.exp(scores - peak_score)
    row_total = jnp.sum(raw_weights, axis=2, keepdims=True)
    weights = raw_weights.astype(jnp.bfloat16)
    mixed_out = (
        jnp.einsum("hsk,khd->hsd", weights, value_heads, preferred_element_type=jnp.float32)
        / row_total
    )
    return jnp.transpose(mixed_out, (1, 0, 2)).reshape(row_count, HEADS * HD)


def shards(
    query,
    keys,
    values,
    hidden,
    latent,
    deal,
    lengths,
    w_out,
    attn_gate,
    modulation,
    w_final,
    guide,
    step_size,
):
    group_id = lax.axis_index("grp")
    branch = lax.axis_index("cfg")
    partner = jnp.bitwise_xor(group_id, 1)
    own_lengths = lax.dynamic_index_in_dim(lengths, group_id, 0, keepdims=False)
    pair_lengths = lax.dynamic_index_in_dim(lengths, partner, 0, keepdims=False)
    item_ids = lax.dynamic_index_in_dim(deal, group_id, 0, keepdims=False)
    resident_key_rows = keys[0, 0]
    local_values = values[0, 0]
    shard_rows = resident_key_rows.shape[1]
    far_keys, far_values = from_partner((resident_key_rows[1], local_values[1]), "grp", 0)
    combined_key_rows, joint_values = (
        lax.all_gather(
            jnp.concatenate([resident_key_rows, far_keys[None]], 0), "seq", axis=1, tiled=True
        ),
        lax.all_gather(
            jnp.concatenate([local_values, far_values[None]], 0), "seq", axis=1, tiled=True
        ),
    )
    group_keys, group_values = (combined_key_rows[:2], joint_values[:2])
    pair_keys, pair_values = (combined_key_rows[2], joint_values[2])
    slot_total = group_keys.shape[1]
    slot_ids = jnp.arange(slot_total)
    live_home = slot_ids < own_lengths[0]
    live_own = slot_ids < own_lengths[1]
    live_pair = slot_ids < pair_lengths[1]
    local_query = query[0, 0]
    local_output_rows = attend(local_query[0], group_keys[0], group_values[0], live_home)
    shared = attend(
        local_query[1],
        jnp.concatenate([group_keys[1], pair_keys], 0),
        jnp.concatenate([group_values[1], pair_values], 0),
        jnp.concatenate([live_own, live_pair], 0),
    )
    attn_rows = (
        jnp.stack([local_output_rows, shared]).astype(jnp.bfloat16).reshape(2 * shard_rows, D)
    )
    projected = jnp.dot(
        attn_rows,
        lax.all_gather(w_out, ("cfg", "seq"), axis=0, tiled=True),
        preferred_element_type=jnp.float32,
    )
    projected = projected.reshape(2, shard_rows, D)
    item_count = guide.shape[0]
    indicator_mask = (jnp.arange(item_count)[None, :] == item_ids[:, None]).astype(jnp.float32)
    gate_now = jnp.einsum(
        "ri,id->rd", indicator_mask, attn_gate[0], precision=lax.Precision.HIGHEST
    )
    stream = hidden[0, 0].astype(jnp.float32) + gate_now[:, None, :] * projected
    row_mean = jnp.mean(stream, axis=2, keepdims=True)
    centred = stream - row_mean
    row_var = jnp.mean(centred * centred, axis=2, keepdims=True)
    normed = centred * lax.rsqrt(row_var + NORM_EPS)
    selected_entries = jnp.einsum(
        "ub,bkg->ukg", indicator_mask, modulation[0], precision=lax.Precision.HIGHEST
    )
    shaped = (
        normed * (1.0 + selected_entries[:, 1][:, None, :]) + selected_entries[:, 0][:, None, :]
    ).astype(jnp.bfloat16)
    velocity = jnp.einsum("rsd,dc->rsc", shaped, w_final, preferred_element_type=jnp.float32)
    row_slots = lax.axis_index("seq") * shard_rows + jnp.arange(shard_rows)
    live_rows = jnp.stack([row_slots < own_lengths[0], row_slots < own_lengths[1]])
    velocity = jnp.where(live_rows[:, :, None], velocity, jnp.float32(0.0))
    weight_now = jnp.sum(indicator_mask * guide[None, :], axis=1)[:, None, None]
    step_now = jnp.sum(indicator_mask * step_size[None, :], axis=1)[:, None, None]
    latent_part = latent[0]
    part_width = latent_part.shape[2]
    outgoing_velocity = lax.dynamic_slice_in_dim(velocity, (1 - branch) * part_width, part_width, 2)
    own_velocity = lax.dynamic_slice_in_dim(velocity, branch * part_width, part_width, 2)
    other_velocity = from_partner(outgoing_velocity, "cfg", 0)
    is_conditional = branch == 0
    cond_velocity = jnp.where(is_conditional, own_velocity, other_velocity)
    uncond_velocity = jnp.where(is_conditional, other_velocity, own_velocity)
    guided = uncond_velocity + weight_now * (cond_velocity - uncond_velocity)
    updated = latent_part - step_now * guided
    return updated[None]


def solution(mesh):
    placed = (
        P("cfg", "grp", None, "seq", None),
        P("cfg", "grp", None, "seq", None),
        P("cfg", "grp", None, "seq", None),
        P("cfg", "grp", None, "seq", None),
        P("grp", None, "seq", "cfg"),
        P(),
        P(),
        P(("cfg", "seq"), None),
        P("cfg", None, None),
        P("cfg", None, None, None),
        P(),
        P(),
        P(),
    )
    return jax.shard_map(
        shards, mesh=mesh, in_specs=placed, out_specs=P("grp", None, "seq", "cfg"), check_vma=False
    )
```

profile of v0, /device:TPU:1, one launch (start us, length us, event | category | flops | bytes accessed | tf_op | source)
XLA Modules:
  0.0 488.3 jit_solution(13304708734672202299)
XLA Ops:
  6.5 0.8 slice_bitcast_fusion.1
  7.3 4.0 collective-permute-start.1
  11.3 0.7 copy.77
  13.1 0.7 slice_bitcast_fusion.2
  13.8 3.4 collective-permute-start
  17.2 0.7 copy.78
  19.0 0.7 all-gather.9.cloned.1.call-update
  19.7 0.7 fusion.67
  20.5 0.8 constant_dynamic-slice_fusion.2
  21.9 0.9 fusion.57
  23.4 0.7 iota_compare_fusion.5
  24.1 1.3 iota_compare_fusion.3
  25.4 1.3 fusion.58
  26.8 1.0 fusion.34
  27.8 1.2 fusion.32
  29.0 122.6 %all-gather.7.cloned.1.call-done = bf16[3,128,2432]{2,0,1:T(4,128)(2,1)} async-done(((bf16[3,2,2432]{2,0,1:T(4,128)(2,1)}), bf16[3,128,2432]{2,0,1:T(4,128)(2,1)}) %all-gather.7.cloned.1.call-update) | async-done | bytes 1867792 | tf_op jit(solution)/shard_map/all_gather | solution.py:65
  151.6 7.6 %fusion.66 = (bf16[1,128,2432]{2,0,1:T(2,128)(2,1)S(1)}, bf16[1,128,2432]{2,0,1:T(2,128)(2,1)}, bf16[1,128,2432]{2,0,1:T(2,128)(2,1)S(1)}) fusion(bf16[3,128,2432]{2,0,1:T(4,128)(2,1)} %all-gather.7.cloned.1.call-done), kind=kLoop, calls=%fused_computation.84 | loop fusion | bytes 3735552 | tf_op jit(solution)/shard_map/slice | solution.py:77
  159.2 2.7 copy.57
  162.0 2.1 copy.56
  164.0 127.7 %all-gather.5.cloned.1.call-done = bf16[3,128,2432]{2,0,1:T(4,128)(2,1)} async-done(((bf16[3,2,2432]{2,0,1:T(4,128)(2,1)}), bf16[3,128,2432]{2,0,1:T(4,128)(2,1)}) %all-gather.5.cloned.1.call-update) | async-done | bytes 1867792 | tf_op jit(solution)/shard_map/all_gather | solution.py:62
  291.8 8.0 %fusion.65 = (bf16[1,128,2432]{2,0,1:T(2,128)(2,1)S(1)}, bf16[1,128,2432]{2,0,1:T(2,128)(2,1)}, bf16[1,128,2432]{2,0,1:T(2,128)(2,1)}) fusion(bf16[3,128,2432]{2,0,1:T(4,128)(2,1)} %all-gather.5.cloned.1.call-done), kind=kLoop, calls=%fused_computation.83 | loop fusion | bytes 3735552 | tf_op jit(solution)/shard_map/slice | solution.py:77
  299.8 3.6 copy.54
  303.4 3.6 copy.53
  306.9 1.7 fusion.69
  309.4 1.4 copy.51
  310.9 1.4 copy.47
  313.4 141.1 %all-gather.9.cloned.1.call-done = bf16[128,19,2432]{2,1,0:T(8,128)(2,1)} async-done(((bf16[1,19,2432]{2,1,0:T(8,128)(2,1)}), bf16[128,19,2432]{2,1,0:T(8,128)(2,1)}) %all-gather.9.cloned.1.call-update) | async-done | bytes 11829264 | tf_op jit(solution)/shard_map/all_gather | solution.py:89
  454.5 16.7 %reshape.76 = bf16[2432,2432,1]{1,0,2:T(8,128)(2,1)} reshape(bf16[128,19,2432]{2,1,0:T(8,128)(2,1)} %all-gather.9.cloned.1.call-done) | data formatting | bytes 23658496
  471.3 6.2 %fusion.71 = (f32[2,2]{1,0:T(2,128)S(1)}, f32[2,2,2432]{2,1,0:T(2,128)S(1)}) fusion(bf16[2432,2432,1]{1,0,2:T(8,128)(2,1)} %reshape.76, bf16[1,2,2432]{2,1,0:T(2,128)(2,1)S(1)} %stack_reshape.9, bf16[1,2,2432]{2,1,0:T(2,128)(2,1)S(1)} %stack_reshape.8, f32[2,2432]{1,0:T(2,128)S(1)} %fusion.34, bf16[1,1,2,2,2432]{4,3,2,1,0:T(2,128)(2,1)S(1)} %copy-done.2), kind=kOutput, calls=%fused_computation.89 | convolution fusion | flops 47394812 | bytes 11926544 | tf_op jit(solution)/shard_map/dot_general | solution.py:87
  478.1 2.2 collective-permute-start.2
  480.4 0.7 collective-permute-done.2
  481.1 0.7 fusion.55
  (45 shorter events, 6.1 us)
Async XLA Ops:
  6.5 471.2 %copy-start = (bf16[2432,64]{0,1:T(8,128)(2,1)S(1)}, bf16[2432,64]{0,1:T(8,128)(2,1)}, u32[]{:S(2)}) copy-start(bf16[2432,64]{0,1:T(8,128)(2,1)} %param.23) | copy-start | bytes 933892
  6.5 145.1 %all-gather.7.cloned.1.call-start = ((), (), s32[]{:S(2)}) async-start(), calls=%async_computation.1 | async-start | bytes 2529280 | tf_op jit(solution)/shard_map/all_gather | solution.py:65
  7.3 5.1 %collective-permute-start.1 = (bf16[2,2432]{1,0:T(2,128)(2,1)S(1)}, bf16[2,2432]{1,0:T(2,128)(2,1)S(1)}, u32[]{:S(2)}, u32[]{:S(2)}) collective-permute-start(bf16[2,2432]{1,0:T(2,128)(2,1)S(1)} %slice_bitcast_fusion.1), channel_id=1, source_target_pairs={{0,64},{64,0},{128,192},{192,128},{1,65},{65,1},{129,193},{193,129... | collective-permute-start | bytes 29192 | tf_op jit(solution)/shard_map/ppermute | solution.py:13
  13.1 278.7 %all-gather.5.cloned.1.call-start = ((), (), s32[]{:S(2)}) async-start(), calls=%async_computation | async-start | bytes 2529280 | tf_op jit(solution)/shard_map/all_gather | solution.py:62
  13.8 4.4 collective-permute-start
  18.9 435.6 %all-gather.9.cloned.1.call-start = ((), (), s32[]{:S(2)}) async-start(), calls=%async_computation.2 | async-start | bytes 15058944 | tf_op jit(solution)/shard_map/all_gather | solution.py:89
  306.9 1.9 copy-start.1
  313.4 157.8 %copy-start.2 = (bf16[1,1,2,2,2432]{4,3,2,1,0:T(2,128)(2,1)S(1)}, bf16[1,1,2,2,2432]{4,3,2,1,0:T(2,128)(2,1)}, u32[]{:S(2)}) copy-start(bf16[1,1,2,2,2432]{4,3,2,1,0:T(2,128)(2,1)} %param.16) | copy-start | bytes 58372
  471.2 9.0 %copy-start.4 = (f32[6]{0:T(128)S(1)}, f32[6]{0:T(128)}, u32[]{:S(2)}) copy-start(f32[6]{0:T(128)} %param.25) | copy-start | bytes 76
  471.2 9.0 %copy-start.5 = (f32[6]{0:T(128)S(1)}, f32[6]{0:T(128)}, u32[]{:S(2)}) copy-start(f32[6]{0:T(128)} %param.24) | copy-start | bytes 76
  471.2 9.9 %copy-start.3 = (f32[1,2,2,32]{3,2,1,0:T(2,128)S(1)}, f32[1,2,2,32]{3,2,1,0:T(2,128)}, u32[]{:S(2)}) copy-start(f32[1,2,2,32]{3,2,1,0:T(2,128)} %param.17) | copy-start | bytes 1540
  478.1 3.1 collective-permute-start.2
Sparse Core Ops, SparseCore 0:
  13.2 138.4 all-gather.6
  154.6 137.1 all-gather.4
  294.8 159.6 all-gather.8
where the time goes:
time: 490 us; the launch traced here: 488 us
  waiting for transfers between devices  393 us (80%)
  local copies, waits for them, and re-layouts  54.1 us (11%)
  between operations  13.3 us (3%)
  matrix products  11.7 us (2%)
  starting transfers between devices  9.63 us (2%)
  other arithmetic  6.06 us (1%)
    all_gather x1, waiting for transfers between devices, shards(): lax.all_gather(w_out, ('cfg', 'seq'), axis=0, tiled=True)  141 us
    all_gather x1, waiting for transfers between devices, shards(): lax.all_gather(jnp.concatenate([resident_key_rows, far_keys[None]], 0), '...  128 us
    all_gather x1, waiting for transfers between devices, shards(): lax.all_gather(jnp.concatenate([local_values, far_values[None]], 0), 'seq...  123 us
    unnamed x15, local copies, waits for them, and re-layouts  18.2 us
  transfers between devices with their start and end apart: 6, of which 6 were waited for; matrix products, arithmetic and copies ran while one was open for 9% of the time, Pallas kernels for 0%

commit v1 on v0

--- a/solution.py
+++ b/solution.py
@@ -7,6 +7,12 @@
 HEADS = 38
 HD = 64
 NORM_EPS = 1e-06
+
+
+def tiled_gather(x, axis, dim):
+    count = lax.axis_size(axis)
+    repeats = [count if d == dim else 1 for d in range(x.ndim)]
+    return lax.all_to_all(jnp.tile(x, repeats), axis, split_axis=dim, concat_axis=dim, tiled=True)
 
 
 def from_partner(x, axis, apart):
@@ -59,9 +65,7 @@
     shard_rows = resident_key_rows.shape[1]
     far_keys, far_values = from_partner((resident_key_rows[1], local_values[1]), "grp", 0)
     combined_key_rows, joint_values = (
-        lax.all_gather(
-            jnp.concatenate([resident_key_rows, far_keys[None]], 0), "seq", axis=1, tiled=True
-        ),
+        tiled_gather(jnp.concatenate([resident_key_rows, far_keys[None]], 0), "seq", 1),
         lax.all_gather(
             jnp.concatenate([local_values, far_values[None]], 0), "seq", axis=1, tiled=True
         ),

time: 490 us -> 375 us (0.77)
  waiting for transfers between devices: 393 us -> 263 us
  starting transfers between devices: 9.63 us -> 27.8 us
    all_gather x1 -> x0, waiting for transfers between devices: 128 us -> none  [shards(): lax.all_gather(jnp.concatenate([resident_key_rows, far_keys[None]], 0), '...]
    all_to_all x0 -> x1, starting transfers between devices: none -> 18.2 us  [tiled_gather(): lax.all_to_all(jnp.tile(x, repeats), axis, split_axis=dim, concat_axis=di...]
    all_gather x1, waiting for transfers between devices: 141 us -> 127 us  [shards(): lax.all_gather(w_out, ('cfg', 'seq'), axis=0, tiled=True)]
    all_gather x1, waiting for transfers between devices: 123 us -> 133 us  [shards(): lax.all_gather(jnp.concatenate([local_values, far_values[None]], 0), 'seq...]
    unnamed x15 -> x31, local copies, waits for them, and re-layouts: 18.2 us -> 18.3 us
  transfers between devices with their start and end apart: 6 -> 6, of which waited for: 6 -> 5; matrix products, arithmetic and copies ran while one was open for 9% -> 11% of each run, Pallas kernels for 0% -> 0%
where the time goes in v1:
time: 375 us; the launch traced here: 374 us
  waiting for transfers between devices  263 us (70%)
  local copies, waits for them, and re-layouts  52.6 us (14%)
  starting transfers between devices  27.8 us (7%)
  between operations  13.7 us (4%)
  matrix products  10.1 us (3%)
  other arithmetic  6.07 us (2%)
    all_gather x1, waiting for transfers between devices, shards(): lax.all_gather(jnp.concatenate([local_values, far_values[None]], 0), 'seq...  133 us
    all_gather x1, waiting for transfers between devices, shards(): lax.all_gather(w_out, ('cfg', 'seq'), axis=0, tiled=True)  127 us
    unnamed x31, local copies, waits for them, and re-layouts  18.3 us
    all_to_all x1, starting transfers between devices, tiled_gather(): lax.all_to_all(jnp.tile(x, repeats), axis, split_axis=dim, concat_axis=di...  18.2 us
    slice x2, local copies, waits for them, and re-layouts, shards(): group_values[0]  10.7 us
    ppermute x3, starting transfers between devices, from_partner(): lax.ppermute(x, axis, [(i, i ^ 1 << apart) for i in range(lax.axis_size(a...  9.55 us
  transfers between devices with their start and end apart: 6, of which 5 were waited for; matrix products, arithmetic and copies ran while one was open for 11% of the time, Pallas kernels for 0%

profile of v1, /device:TPU:1, one launch (start us, length us, event | category | flops | bytes accessed | tf_op | source)
XLA Modules:
  0.0 373.6 jit_solution(11829988478759540813)
XLA Ops:
  6.5 0.8 slice_bitcast_fusion.1
  7.3 4.0 %collective-permute-start.1 = (bf16[2,2432]{1,0:T(2,128)(2,1)S(1)}, bf16[2,2432]{1,0:T(2,128)(2,1)S(1)}, u32[]{:S(2)}, u32[]{:S(2)}) collective-permute-start(bf16[2,2432]{1,0:T(2,128)(2,1)S(1)} %slice_bitcast_fusion.1), channel_id=1, source_target_pairs={{0,64},{64,0},{128,192},{192,128},{1,65},{65,1},{129,193},{193,129... | collective-permute-start | bytes 29192 | tf_op jit(solution)/shard_map/ppermute | solution.py:19
  11.3 0.7 copy.75
  12.4 0.7 pad_maximum_fusion
  13.1 0.7 all-gather.6.cloned.1.call-update
  13.8 0.7 slice_bitcast_fusion.2
  14.5 3.4 collective-permute-start
  17.9 1.4 collective-permute-done
  19.3 0.8 pad_maximum_fusion.1
  20.1 2.1 tile.4.clone
  22.2 18.2 %all-to-all-start = ((bf16[3,128,2432]{2,0,1:T(4,128)(2,1)}), bf16[3,128,2432]{2,0,1:T(4,128)(2,1)S(1)}, u32[]{:S(2)}, u32[]{:S(2)}) async-start(bf16[3,128,2432]{2,0,1:T(4,128)(2,1)} %bitcast.65), calls=%async_computation | async-start | bytes 4980736 | tf_op jit(solution)/shard_map/all_to_all | solution.py:15
  41.5 0.6 fusion.68
  42.0 0.6 iota_compare_fusion.5
  42.7 1.3 iota_compare_fusion.3
  44.0 1.3 fusion.58
  45.8 133.1 %all-gather.4.cloned.1.call-done = bf16[3,128,2432]{2,0,1:T(4,128)(2,1)} async-done(((bf16[3,2,2432]{2,0,1:T(4,128)(2,1)}), bf16[3,128,2432]{2,0,1:T(4,128)(2,1)}) %all-gather.4.cloned.1.call-update) | async-done | bytes 1867792 | tf_op jit(solution)/shard_map/all_gather | solution.py:69
  178.9 8.0 %fusion.66 = (bf16[1,128,2432]{2,0,1:T(2,128)(2,1)}, bf16[1,128,2432]{2,0,1:T(2,128)(2,1)}, bf16[1,128,2432]{2,0,1:T(2,128)(2,1)}) fusion(bf16[3,128,2432]{2,0,1:T(4,128)(2,1)} %all-gather.4.cloned.1.call-done), kind=kLoop, calls=%fused_computation.83 | loop fusion | bytes 3735552 | tf_op jit(solution)/shard_map/slice | solution.py:81
  186.9 3.6 copy.54
  190.4 3.6 copy.53
  194.1 2.7 copy.48
  196.8 3.8 %fusion.65 = (bf16[1,128,2432]{2,0,1:T(2,128)(2,1)}, bf16[1,128,2432]{2,0,1:T(2,128)(2,1)}, bf16[1,128,2432]{2,0,1:T(2,128)(2,1)}) fusion(bf16[3,128,2432]{2,0,1:T(4,128)(2,1)S(1)} %all-to-all-done), kind=kLoop, calls=%fused_computation.82 | loop fusion | bytes 3735552 | tf_op jit(solution)/shard_map/slice | solution.py:81
  200.7 3.7 copy.51
  204.4 2.0 copy.50
  206.4 1.7 fusion.69
  209.0 0.7 copy-done.1
  209.7 1.4 copy.44
  212.2 127.2 %all-gather.6.cloned.1.call-done = bf16[128,19,2432]{2,1,0:T(8,128)(2,1)} async-done(((bf16[1,19,2432]{2,1,0:T(8,128)(2,1)}), bf16[128,19,2432]{2,1,0:T(8,128)(2,1)}) %all-gather.6.cloned.1.call-update) | async-done | bytes 11829264 | tf_op jit(solution)/shard_map/all_gather | solution.py:93
  339.4 16.8 %reshape.80 = bf16[2432,2432,1]{1,0,2:T(8,128)(2,1)} reshape(bf16[128,19,2432]{2,1,0:T(8,128)(2,1)} %all-gather.6.cloned.1.call-done) | data formatting | bytes 23658496
  356.2 6.2 %fusion.71 = (f32[2,2]{1,0:T(2,128)S(1)}, f32[2,2,2432]{2,1,0:T(2,128)S(1)}) fusion(bf16[2432,2432,1]{1,0,2:T(8,128)(2,1)} %reshape.80, bf16[1,2,2432]{2,1,0:T(2,128)(2,1)S(1)} %stack_reshape.9, bf16[1,2,2432]{2,1,0:T(2,128)(2,1)S(1)} %stack_reshape.8, f32[2,2432]{1,0:T(2,128)S(1)} %fusion.34, bf16[1,1,2,2,2432]{4,3,2,1,0:T(2,128)(2,1)S(1)} %copy-done.7), kind=kOutput, calls=%fused_computation.88 | convolution fusion | flops 47394812 | bytes 11926544 | tf_op jit(solution)/shard_map/dot_general | solution.py:91
  363.0 2.2 collective-permute-start.2
  365.4 0.7 collective-permute-done.2
  366.1 0.7 fusion.55
  (60 shorter events, 4.6 us)
Async XLA Ops:
  6.5 356.1 %copy-start = (bf16[2432,64]{0,1:T(8,128)(2,1)S(1)}, bf16[2432,64]{0,1:T(8,128)(2,1)}, u32[]{:S(2)}) copy-start(bf16[2432,64]{0,1:T(8,128)(2,1)} %param.23) | copy-start | bytes 933892
  6.5 172.3 %all-gather.4.cloned.1.call-start = ((), (), s32[]{:S(2)}) async-start(), calls=%async_computation.1 | async-start | bytes 2529280 | tf_op jit(solution)/shard_map/all_gather | solution.py:69
  7.3 5.1 %collective-permute-start.1 = (bf16[2,2432]{1,0:T(2,128)(2,1)S(1)}, bf16[2,2432]{1,0:T(2,128)(2,1)S(1)}, u32[]{:S(2)}, u32[]{:S(2)}) collective-permute-start(bf16[2,2432]{1,0:T(2,128)(2,1)S(1)} %slice_bitcast_fusion.1), channel_id=1, source_target_pairs={{0,64},{64,0},{128,192},{192,128},{1,65},{65,1},{129,193},{193,129... | collective-permute-start | bytes 29192 | tf_op jit(solution)/shard_map/ppermute | solution.py:19
  13.1 326.4 %all-gather.6.cloned.1.call-start = ((), (), s32[]{:S(2)}) async-start(), calls=%async_computation.2 | async-start | bytes 15058944 | tf_op jit(solution)/shard_map/all_gather | solution.py:93
  14.5 4.7 %collective-permute-start = (bf16[2,2432]{1,0:T(2,128)(2,1)S(1)}, bf16[2,2432]{1,0:T(2,128)(2,1)S(1)}, u32[]{:S(2)}, u32[]{:S(2)}) collective-permute-start(bf16[2,2432]{1,0:T(2,128)(2,1)S(1)} %slice_bitcast_fusion.2), channel_id=1, source_target_pairs={{0,64},{64,0},{128,192},{192,128},{1,65},{65,1},{129,193},{193,129... | collective-permute-start | bytes 29192 | tf_op jit(solution)/shard_map/ppermute | solution.py:19
  22.1 18.3 %copy-start.8 = (bf16[1,1,2,2,2432]{4,3,2,1,0:T(2,128)(2,1)S(1)}, bf16[1,1,2,2,2432]{4,3,2,1,0:T(2,128)(2,1)}, u32[]{:S(2)}) copy-start(bf16[1,1,2,2,2432]{4,3,2,1,0:T(2,128)(2,1)} %param.13) | copy-start | bytes 58372
  22.1 18.4 %copy-start.9 = (s32[4,2]{0,1:T(2,128)S(1)}, s32[4,2]{0,1:T(2,128)}, u32[]{:S(2)}) copy-start(s32[4,2]{0,1:T(2,128)} %param.19) | copy-start | bytes 100
  22.1 19.1 %copy-start.11 = (s32[4,2]{0,1:T(2,128)S(1)}, s32[4,2]{0,1:T(2,128)}, u32[]{:S(2)}) copy-start(s32[4,2]{0,1:T(2,128)} %param.18) | copy-start | bytes 100
  22.1 23.1 %copy-start.6 = (f32[1,6,2432]{2,0,1:T(1,128)S(1)}, f32[1,6,2432]{2,0,1:T(1,128)}, u32[]{:S(2)}) copy-start(f32[1,6,2432]{2,0,1:T(1,128)} %param.21) | copy-start | bytes 175108
  22.1 23.4 %copy-start.5 = (f32[1,6,2,2432]{3,2,1,0:T(2,128)S(1)}, f32[1,6,2,2432]{3,2,1,0:T(2,128)}, u32[]{:S(2)}) copy-start(f32[1,6,2,2432]{3,2,1,0:T(2,128)} %param.22) | copy-start | bytes 350212
  22.2 174.6 %all-to-all-start = ((bf16[3,128,2432]{2,0,1:T(4,128)(2,1)}), bf16[3,128,2432]{2,0,1:T(4,128)(2,1)S(1)}, u32[]{:S(2)}, u32[]{:S(2)}) async-start(bf16[3,128,2432]{2,0,1:T(4,128)(2,1)} %bitcast.65), calls=%async_computation | async-start | bytes 4980736 | tf_op jit(solution)/shard_map/all_to_all | solution.py:15
  200.7 3.7 copy-start.2
  206.4 1.9 copy-start.3
  206.4 1.9 copy-start.4
  208.4 1.3 copy-start.1
  212.2 144.0 %copy-start.7 = (bf16[1,1,2,2,2432]{4,3,2,1,0:T(2,128)(2,1)S(1)}, bf16[1,1,2,2,2432]{4,3,2,1,0:T(2,128)(2,1)}, u32[]{:S(2)}) copy-start(bf16[1,1,2,2,2432]{4,3,2,1,0:T(2,128)(2,1)} %param.16) | copy-start | bytes 58372
  356.2 9.0 %copy-start.12 = (f32[6]{0:T(128)S(1)}, f32[6]{0:T(128)}, u32[]{:S(2)}) copy-start(f32[6]{0:T(128)} %param.25) | copy-start | bytes 76
  356.2 9.0 %copy-start.13 = (f32[6]{0:T(128)S(1)}, f32[6]{0:T(128)}, u32[]{:S(2)}) copy-start(f32[6]{0:T(128)} %param.24) | copy-start | bytes 76
  356.2 9.9 %copy-start.10 = (f32[1,2,2,32]{3,2,1,0:T(2,128)S(1)}, f32[1,2,2,32]{3,2,1,0:T(2,128)}, u32[]{:S(2)}) copy-start(f32[1,2,2,32]{3,2,1,0:T(2,128)} %param.17) | copy-start | bytes 1540
  363.0 3.1 collective-permute-start.2
Sparse Core Ops, SparseCore 0:
  13.2 165.6 all-gather.3
  181.9 157.4 all-gather.5
